TPU v7x, 32 devices: a whole 2x2x4 slice. The times are simulated.
32 devices in a mesh: layer: 4 (over x, core), tok: 8 (over z, y).
Axes of the slice: x: 2, y: 2, z: 4, core: 2. Of those that a mesh axis runs over, the one named last changes fastest.
Arguments:
- active_codes: bfloat16 [4, 1024, 32], P('layer', 'tok'), may hold values from 0.19921875 to 3
- latent_ids: int32 [4, 1024, 32], P('layer', 'tok'), may hold values from 0 to 32767, as said below
- decoder: bfloat16 [4, 32768, 4096], P('layer', 'tok'), may hold values from -1 to 1
- carry_gain: float32 [4, 4096], P('layer'), may hold values from 0.1 to 1
- earlier_sum: bfloat16 [1024, 4096], P('tok'), may hold values from -6 to 6
- targets: bfloat16 [4, 1024, 4096], P('layer', 'tok'), may hold values from -6 to 6
Outputs:
- reconstruction: bfloat16 [4, 1024, 4096], P('layer', 'tok')
- code_grad: float32 [4, 1024, 32], P('layer', 'tok')
Inputs may be any that keep to these rules, and one draw needn't show every extreme that they name: `latent_ids`: A token's 32 ids in one layer are distinct. In each layer, the 128 tokens of one aligned block have at most 768 ids in any one range of 4096 consecutive latents, and in every layer one range holds exactly 768 ids of every block.
All inputs are finite; a program needn't handle non-finite values.
Results may differ from a plain program's by a relative error of at most 0.019.
Values may be sent and summed in bfloat16 or wider, within the bound.
No kernel may reach another device: no remote copies, remote signals or barrier semaphores. Data moves between devices by JAX's collectives and lax.ppermute only.
A program may use at most 256 MiB of HBM per device.

v0:
```python
import jax
import jax.numpy as jnp
from jax import lax
from jax.sharding import PartitionSpec as P

LANES = 128


def selectors(ids_all, range_size):
    base = lax.axis_index("tok") * range_size
    local = ids_all - base
    inside = (local >= 0) & (local < range_size)
    high = jnp.where(inside, local // LANES, -1)
    low = local % LANES
    high_hot = high[..., None] == jnp.arange(range_size // LANES, dtype=jnp.int32)
    low_hot = low[..., None] == jnp.arange(LANES, dtype=jnp.int32)
    return (high_hot, low_hot)


def exchange_codes(latent_ids, active_codes):
    owners = lax.axis_size("tok")
    top_count = latent_ids.shape[1]
    packed = jnp.concatenate(
        [
            (latent_ids // 256).astype(jnp.bfloat16),
            (latent_ids % 256).astype(jnp.bfloat16),
            active_codes,
        ],
        axis=1,
    )
    spread = jnp.broadcast_to(packed[None], (owners,) + packed.shape)
    gathered = lax.all_to_all(spread, "tok", split_axis=0, concat_axis=0, tiled=True)
    gathered = gathered.reshape(-1, 3 * top_count)
    ids_all = gathered[:, :top_count].astype(jnp.int32) * 256 + gathered[
        :, top_count : 2 * top_count
    ].astype(jnp.int32)
    codes_all = gathered[:, 2 * top_count :]
    return (ids_all, codes_all)


def layer_chain(decoded, carry_gain, earlier_sum, targets):
    gains = lax.all_gather(carry_gain[0], "layer", axis=0, tiled=False)
    targets_all = lax.all_gather(targets[0], "layer", axis=0, tiled=False)
    decoded_all = lax.all_gather(decoded.astype(jnp.bfloat16), "layer", axis=0, tiled=False)
    layers = gains.shape[0]
    me = lax.axis_index("layer")
    carried = earlier_sum.astype(jnp.float32)
    misfits = []
    recon_own = jnp.zeros_like(decoded)
    for m in range(layers):
        own = me == m
        term = jnp.where(own, decoded, decoded_all[m].astype(jnp.float32))
        carried = term + gains[m][None, :] * carried
        recon_own = jnp.where(own, carried, recon_own)
        misfits.append(carried - targets_all[m].astype(jnp.float32))
    running = misfits[layers - 1]
    grad_own = jnp.where(me == layers - 1, running, jnp.zeros_like(running))
    for m in range(layers - 2, -1, -1):
        running = misfits[m] + gains[m + 1][None, :] * running
        grad_own = jnp.where(me == m, running, grad_own)
    return (recon_own, grad_own)


def on_device(active_codes, latent_ids, decoder, carry_gain, earlier_sum, targets):
    range_size = decoder.shape[1]
    owners = lax.axis_size("tok")
    weights = decoder[0]
    ids_all, codes_all = exchange_codes(latent_ids[0], active_codes[0])
    tokens = ids_all.shape[0]
    high_hot, low_hot = selectors(ids_all, range_size)
    coded_high = jnp.where(high_hot, codes_all[..., None], jnp.zeros((), jnp.bfloat16))
    spread = jnp.einsum(
        "tkh,tkl->thl", coded_high, low_hot.astype(jnp.bfloat16), preferred_element_type=jnp.float32
    )
    spread = spread.astype(jnp.bfloat16).reshape(tokens, range_size)
    half = weights.shape[1] // 2
    w_first, w_second = (weights[:, :half], weights[:, half:])
    partial_first = jnp.dot(spread, w_first, preferred_element_type=jnp.float32).astype(
        jnp.bfloat16
    )
    decoded_first = lax.psum_scatter(partial_first, "tok", scatter_dimension=0, tiled=True)
    partial_second = jnp.dot(spread, w_second, preferred_element_type=jnp.float32).astype(
        jnp.bfloat16
    )
    received = lax.all_to_all(partial_second, "tok", split_axis=0, concat_axis=0, tiled=True)
    decoded_second = jnp.sum(
        received.reshape(owners, -1, received.shape[1]).astype(jnp.float32), axis=0
    )
    decoded = jnp.concatenate([decoded_first.astype(jnp.float32), decoded_second], axis=1)
    recon_full, grad_sum = layer_chain(decoded, carry_gain, earlier_sum, targets)
    grad_low = grad_sum.astype(jnp.bfloat16)
    segment = lax.all_gather(grad_low, "tok", axis=0, tiled=True)
    products = lax.dot_general(
        segment, weights, (((1,), (1,)), ((), ())), preferred_element_type=jnp.float32
    ).astype(jnp.bfloat16)
    products = products.reshape(tokens, range_size // LANES, LANES)
    picked_low = jnp.einsum(
        "thl,tkl->tkh", products, low_hot.astype(jnp.bfloat16), preferred_element_type=jnp.float32
    )
    partial_grad = jnp.sum(jnp.where(high_hot, picked_low, 0.0), axis=-1)
    returned = lax.all_to_all(partial_grad, "tok", split_axis=0, concat_axis=0, tiled=True)
    code_grad = jnp.sum(returned.reshape(owners, -1, returned.shape[1]), axis=0)
    return (recon_full.astype(jnp.bfloat16)[None], code_grad[None])


def solution(mesh):
    return jax.shard_map(
        on_device,
        mesh=mesh,
        in_specs=(
            P("layer", "tok", None),
            P("layer", "tok", None),
            P("layer", "tok", None),
            P("layer", None),
            P("tok", None),
            P("layer", "tok", None),
        ),
        out_specs=(P("layer", "tok", None), P("layer", "tok", None)),
        check_vma=False,
    )
```

profile of v0, /device:TPU:0, one launch (start us, length us, event | category | flops | bytes accessed | tf_op | source)
XLA Modules:
  0.0 465.8 jit_solution(1806440239437753471)
XLA Ops:
  8.0 0.7 fusion.42
  8.7 0.7 pad_maximum_fusion.2
  9.4 0.7 broadcast_in_dim.35
  10.1 7.3 %all-to-all-start = ((bf16[8,128,96]{1,2,0:T(8,128)(2,1)}), bf16[8,128,96]{1,2,0:T(8,128)(2,1)S(1)}, u32[]{:S(2)}, u32[]{:S(2)}) async-start(bf16[8,128,96]{1,2,0:T(8,128)(2,1)} %broadcast_in_dim.35), calls=%async_computation | async-start | bytes 393216 | tf_op jit(solution)/shard_map/all_to_all | solution.py:32
  17.4 0.0 reduce-scatter.2.cloned.1.call-start
  17.5 7.9 %all-to-all-done = bf16[8,128,96]{1,2,0:T(8,128)(2,1)S(1)} async-done(((bf16[8,128,96]{1,2,0:T(8,128)(2,1)}), bf16[8,128,96]{1,2,0:T(8,128)(2,1)S(1)}, u32[]{:S(2)}, u32[]{:S(2)}) %all-to-all-start) | async-done | bytes 196640 | tf_op jit(solution)/shard_map/all_to_all | solution.py:32
  25.4 0.2 fusion.40
  25.6 0.2 copy.17
  25.8 0.0 copy-start.1
  25.8 0.2 copy.15
  26.0 0.0 copy-start.3
  26.0 0.2 copy.16
  26.2 9.7 %fusion.15 = bf16[1024,32,128]{2,1,0:T(8,128)(2,1)S(1)} fusion(s32[1024,32]{1,0:T(8,128)S(1)} %copy.17, s32[1024,32]{1,0:T(8,128)S(1)} %copy.15, bf16[1024,32]{1,0:T(8,128)(2,1)S(1)} %copy.16), kind=kOutput, calls=%fused_computation.19 | convolution fusion | flops 278921216 | bytes 8716288 | tf_op jit(solution)/shard_map/tkh,tkl->thl/dot_general | solution.py:72
  35.9 0.0 copy-done.1
  35.9 0.0 copy-done.3
  35.9 0.0 copy-start.6
  35.9 3.3 copy-done.6
  39.3 21.9 %fusion.20 = bf16[1024,2048]{1,0:T(8,128)(2,1)} fusion(bf16[4096,4096]{1,0:T(8,128)(2,1)} %bitcast.126, bf16[128,8,32,128]{3,2,1,0:T(8,128)(2,1)S(1)} %bitcast.128), kind=kOutput, calls=%fused_computation.22 | convolution fusion | flops 17181966336 | bytes 29360128 | tf_op jit(solution)/shard_map/dot_general | solution.py:78
  61.1 0.0 reduce-scatter.2.cloned.1.call-update
  61.1 24.0 %fusion.25 = bf16[1024,2048]{1,0:T(8,128)(2,1)} fusion(bf16[4096,4096]{1,0:T(8,128)(2,1)} %bitcast.127, bf16[128,8,32,128]{3,2,1,0:T(8,128)(2,1)} %bitcast.129), kind=kOutput, calls=%fused_computation.23 | convolution fusion | flops 17181966336 | bytes 29360128 | tf_op jit(solution)/shard_map/dot_general | solution.py:82
  85.2 4.6 all-to-all-start.1
  89.7 0.0 all-gather.7.cloned.1.call-start
  89.8 0.5 all-gather.7.cloned.1.call-update
  90.3 0.0 all-gather.5.cloned.1.call-start
  90.4 103.3 %all-to-all-done.1 = bf16[8,128,2048]{2,1,0:T(8,128)(2,1)} async-done(((bf16[8,128,2048]{2,1,0:T(8,128)(2,1)}), bf16[8,128,2048]{2,1,0:T(8,128)(2,1)}, u32[]{:S(2)}, u32[]{:S(2)}) %all-to-all-start.1) | async-done | bytes 4194336 | tf_op jit(solution)/shard_map/all_to_all | solution.py:85
  193.6 3.4 convert_reduce_fusion
  197.0 0.0 copy-start.5
  197.0 0.1 convert_bitcast_fusion.1
  197.1 18.2 %reduce-scatter.2.cloned.1.call-done = bf16[128,2048]{1,0:T(8,128)(2,1)} async-done(((bf16[1024,2048]{1,0:T(8,128)(2,1)}), bf16[128,2048]{1,0:T(8,128)(2,1)}) %reduce-scatter.2.cloned.1.call-update) | async-done | bytes 524304 | tf_op jit(solution)/shard_map/reduce_scatter | solution.py:81
  215.3 0.0 copy-start
  215.3 2.2 pad_maximum_fusion.1
  217.5 0.0 all-gather.5.cloned.1.call-update
  217.5 0.0 all-gather.9.cloned.1.call-start
  217.6 0.0 copy-done.5
  217.6 5.4 %all-gather = f32[4,1,4096]{2,1,0:T(1,128)S(1)} all-gather(f32[1,1,4096]{2,1,0:T(1,128)S(1)} %bitcast.123), channel_id=1, replica_groups=mesh['layer'=4,'tok'=8] {'layer'}, dimensions={0}, use_global_device_ids=true | all-gather | bytes 81920 | tf_op jit(solution)/shard_map/all_gather | solution.py:42
  223.0 1.2 convert_element_type.103
  224.2 0.0 all-gather.7.cloned.1.call-done
  224.3 27.4 %all-gather.5.cloned.1.call-done = bf16[4,128,4096]{2,1,0:T(8,128)(2,1)} async-done(((bf16[1,128,4096]{2,1,0:T(8,128)(2,1)}), bf16[4,128,4096]{2,1,0:T(8,128)(2,1)}) %all-gather.5.cloned.1.call-update) | async-done | bytes 4194320 | tf_op jit(solution)/shard_map/all_gather | solution.py:44
  251.7 0.0 copy-done
  251.7 5.4 %fusion.34 = bf16[128,4096]{1,0:T(8,128)(2,1)} fusion(bf16[128,4096]{1,0:T(8,128)(2,1)S(1)} %copy-done, f32[128,2048]{1,0:T(8,128)S(1)} %convert_reduce_fusion, f32[128,2048]{1,0:T(8,128)S(1)} %convert_element_type.103, bf16[4,128,4096]{2,1,0:T(8,128)(2,1)} %all-gather.7.cloned.1.call-done, f32[4096]{0:T(1024)S(1)} %bitcast.121, f32[4096]{0:T(1024)S(1)} %bitcast.117, ...), kind=kLoop, calls=%fused_computation.33 | loop fusion | flops 19398656 | bytes 12648452 | tf_op jit(solution)/shard_map/convert_element_type | solution.py:91
  257.1 0.0 all-gather.9.cloned.1.call-update
  257.1 125.1 %all-gather.9.cloned.1.call-done = bf16[1024,4096]{1,0:T(8,128)(2,1)} async-done(((bf16[128,4096]{1,0:T(8,128)(2,1)}), bf16[1024,4096]{1,0:T(8,128)(2,1)}) %all-gather.9.cloned.1.call-update) | async-done | bytes 8388624 | tf_op jit(solution)/shard_map/all_gather | solution.py:92
  382.2 42.6 %convert_bitcast_fusion = bf16[128,8,32,128]{3,1,2,0:T(8,128)(2,1)} fusion(bf16[1024,4096]{1,0:T(8,128)(2,1)} %all-gather.9.cloned.1.call-done, bf16[1,4096,4096]{2,1,0:T(8,128)(2,1)} %param.8), kind=kOutput, calls=%fused_computation.12 | convolution fusion | flops 34363932672 | bytes 50331648 | tf_op jit(solution)/shard_map/dot_general | solution.py:93
  424.8 0.0 copy-start.2
  424.8 0.0 copy-start.4
  424.8 9.7 %copy.24 = bf16[128,8,32,128]{3,2,1,0:T(8,128)(2,1)} copy(bf16[128,8,32,128]{3,1,2,0:T(8,128)(2,1)} %convert_bitcast_fusion) | data formatting | bytes 16777216
  434.5 0.0 copy-done.2
  434.5 0.0 copy-done.4
  434.5 10.7 %select_reduce_fusion = f32[1024,32]{1,0:T(8,128)} fusion(s32[1024,32]{1,0:T(8,128)S(1)} %copy-done.4, bf16[1024,32,128]{2,1,0:T(8,128)(2,1)} %bitcast.111, s32[1024,32]{1,0:T(8,128)S(1)} %copy-done.2), kind=kOutput, calls=%fused_computation.4 | convolution fusion | flops 275742720 | bytes 8781824 | tf_op jit(solution)/shard_map/thl,tkl->tkh/dot_general | solution.py:97
  445.2 1.9 copy.19
  447.1 3.4 all-to-all-start.2
  450.5 3.8 fusion.39
  454.3 3.5 all-to-all-done.2
  457.7 0.6 reduce_sum.29
  (3 shorter events, 0.0 us)
Async XLA Ops:
  10.1 15.2 %all-to-all-start = ((bf16[8,128,96]{1,2,0:T(8,128)(2,1)}), bf16[8,128,96]{1,2,0:T(8,128)(2,1)S(1)}, u32[]{:S(2)}, u32[]{:S(2)}) async-start(bf16[8,128,96]{1,2,0:T(8,128)(2,1)} %broadcast_in_dim.35), calls=%async_computation | async-start | bytes 393216 | tf_op jit(solution)/shard_map/all_to_all | solution.py:32
  17.4 197.9 %reduce-scatter.2.cloned.1.call-start = ((), (), s32[]{:S(2)}) async-start(), calls=%async_computation.4 | async-start | bytes 4718592 | tf_op jit(solution)/shard_map/reduce_scatter | solution.py:81
  25.8 10.1 %copy-start.1 = (s32[1024,32]{1,0:T(8,128)}, s32[1024,32]{1,0:T(8,128)S(1)}, u32[]{:S(2)}) copy-start(s32[1024,32]{1,0:T(8,128)S(1)} %copy.17) | copy-start | bytes 393220
  26.0 9.9 %copy-start.3 = (s32[1024,32]{1,0:T(8,128)}, s32[1024,32]{1,0:T(8,128)S(1)}, u32[]{:S(2)}) copy-start(s32[1024,32]{1,0:T(8,128)S(1)} %copy.15) | copy-start | bytes 393220
  35.9 3.3 copy-start.6
  85.2 108.5 %all-to-all-start.1 = ((bf16[8,128,2048]{2,1,0:T(8,128)(2,1)}), bf16[8,128,2048]{2,1,0:T(8,128)(2,1)}, u32[]{:S(2)}, u32[]{:S(2)}) async-start(bf16[8,128,2048]{2,1,0:T(8,128)(2,1)} %bitcast.112), calls=%async_computation.2 | async-start | bytes 8388608 | tf_op jit(solution)/shard_map/all_to_all | solution.py:85
  89.7 134.5 %all-gather.7.cloned.1.call-start = ((), (), s32[]{:S(2)}) async-start(), calls=%async_computation.6 | async-start | bytes 5242880 | tf_op jit(solution)/shard_map/all_gather | solution.py:43
  90.3 161.4 %all-gather.5.cloned.1.call-start = ((), (), s32[]{:S(2)}) async-start(), calls=%async_computation.5 | async-start | bytes 5242880 | tf_op jit(solution)/shard_map/all_gather | solution.py:44
  197.0 20.6 %copy-start.5 = (f32[1,4096]{1,0:T(1,128)S(1)}, f32[1,4096]{1,0:T(1,128)}, u32[]{:S(2)}) copy-start(f32[1,4096]{1,0:T(1,128)} %param.9) | copy-start | bytes 49156
  215.3 36.4 %copy-start = (bf16[128,4096]{1,0:T(8,128)(2,1)S(1)}, bf16[128,4096]{1,0:T(8,128)(2,1)}, u32[]{:S(2)}) copy-start(bf16[128,4096]{1,0:T(8,128)(2,1)} %param.10) | copy-start | bytes 3145732
  217.5 164.7 %all-gather.9.cloned.1.call-start = ((), (), s32[]{:S(2)}) async-start(), calls=%async_computation.7 | async-start | bytes 9437184 | tf_op jit(solution)/shard_map/all_gather | solution.py:92
  424.8 9.7 %copy-start.2 = (s32[1024,32]{1,0:T(8,128)S(1)}, s32[1024,32]{1,0:T(8,128)}, u32[]{:S(2)}) copy-start(s32[1024,32]{1,0:T(8,128)} %copy-done.1) | copy-start | bytes 393220
  424.8 9.7 %copy-start.4 = (s32[1024,32]{1,0:T(8,128)S(1)}, s32[1024,32]{1,0:T(8,128)}, u32[]{:S(2)}) copy-start(s32[1024,32]{1,0:T(8,128)} %copy-done.3) | copy-start | bytes 393220
  447.1 10.7 %all-to-all-start.2 = ((f32[8,128,32]{1,2,0:T(8,128)}), f32[8,128,32]{1,2,0:T(8,128)S(1)}, u32[]{:S(2)}, u32[]{:S(2)}) async-start(f32[8,128,32]{1,2,0:T(8,128)} %copy.19), calls=%async_computation.3 | async-start | bytes 262144 | tf_op jit(solution)/shard_map/all_to_all | solution.py:101
Sparse Core Ops, SparseCore 0:
  61.3 154.0 reduce-scatter.1
  257.3 124.9 all-gather.8
Sparse Core Ops, SparseCore 1:
  91.9 35.6 all-gather.6
  217.6 34.0 all-gather.4
where the time goes:
time: 466 us
  waiting for transfers between devices  286 us (61%)
  matrix products  109 us (23%)
  other arithmetic  18.2 us (4%)
  local copies, waits for them, and re-layouts  16.2 us (3%)
  between operations  15.7 us (3%)
  starting transfers between devices  15.4 us (3%)
  blocking collectives  5.43 us (1%)
    all_gather x1, waiting for transfers between devices, on_device(): segment = lax.all_gather(grad_low, 'tok', axis=0, tiled=True)  125 us
    all_to_all x1, waiting for transfers between devices, on_device(): lax.all_to_all(partial_second, 'tok', split_axis=0, concat_axis=0, tiled=...  103 us
    dot_general x1, matrix products, on_device(): lax.dot_general(segment, weights, (((1,), (1,)), ((), ())), preferred_ele...  42.6 us
    all_gather x1, waiting for transfers between devices, layer_chain(): lax.all_gather(decoded.astype(jnp.bfloat16), 'layer', axis=0, tiled=False)  27.4 us
    dot_general x1, matrix products, on_device(): jnp.dot(spread, w_second, preferred_element_type=jnp.float32)  24 us
    dot_general x1, matrix products, on_device(): jnp.dot(spread, w_first, preferred_element_type=jnp.float32)  21.9 us
    reduce_scatter x1, waiting for transfers between devices, on_device(): lax.psum_scatter(partial_first, 'tok', scatter_dimension=0, tiled=True)  18.2 us
    unnamed x15, local copies, waits for them, and re-layouts  13 us
  transfers between devices with their start and end apart: 7, of which 6 were waited for; matrix products, arithmetic and copies ran while one was open for 7% of the time, Pallas kernels for 0%

commit v1 on v0

--- a/solution.py
+++ b/solution.py
@@ -4,6 +4,12 @@
 from jax.sharding import PartitionSpec as P
 
 LANES = 128
+
+
+def joined_along(blocks, dim):
+    lengths = list(blocks.shape[1:])
+    lengths[dim] *= blocks.shape[0]
+    return jnp.moveaxis(blocks, 0, dim).reshape(lengths)
 
 
 def selectors(ids_all, range_size):
@@ -89,7 +95,14 @@
     decoded = jnp.concatenate([decoded_first.astype(jnp.float32), decoded_second], axis=1)
     recon_full, grad_sum = layer_chain(decoded, carry_gain, earlier_sum, targets)
     grad_low = grad_sum.astype(jnp.bfloat16)
-    segment = lax.all_gather(grad_low, "tok", axis=0, tiled=True)
+    length = lax.axis_size("tok")
+    right = [(i, (i + 1) % length) for i in range(length)]
+    pieces = [grad_low]
+    while len(pieces) < length:
+        pieces.append(lax.ppermute(pieces[-1], "tok", right))
+    mine = lax.axis_index("tok")
+    pieces = jnp.stack(pieces)[(mine - jnp.arange(length)) % length]
+    segment = joined_along(pieces, 0)
     products = lax.dot_general(
         segment, weights, (((1,), (1,)), ((), ())), preferred_element_type=jnp.float32
     ).astype(jnp.bfloat16)

time: 466 us -> 528 us (1.13)
  waiting for transfers between devices: 286 us -> 331 us
  local copies, waits for them, and re-layouts: 16.2 us -> 31.4 us
    ppermute x0 -> x7, waiting for transfers between devices: none -> 170 us  [on_device(): pieces.append(lax.ppermute(pieces[-1], 'tok', right))]
    all_gather x1 -> x0, waiting for transfers between devices: 125 us -> none  [on_device(): segment = lax.all_gather(grad_low, 'tok', axis=0, tiled=True)]
    gather x0 -> x1, local copies, waits for them, and re-layouts: none -> 8.06 us  [on_device(): pieces = jnp.stack(pieces)[(mine - jnp.arange(length)) % length]]
    unnamed x15 -> x21, local copies, waits for them, and re-layouts: 13 us -> 19.1 us
    unnamed x0 -> x1, other arithmetic: none -> 5.4 us
    convert_element_type x1 -> x0, other arithmetic: 5.4 us -> none  [on_device(): grad_low = grad_sum.astype(jnp.bfloat16)]
  transfers between devices with their start and end apart: 7 -> 13, of which waited for: 6 -> 12; matrix products, arithmetic and copies ran while one was open for 7% -> 8% of each run, Pallas kernels for 0% -> 0%
where the time goes in v1:
time: 528 us; the launch traced here: 527 us
  waiting for transfers between devices  331 us (63%)
  matrix products  109 us (21%)
  local copies, waits for them, and re-layouts  31.4 us (6%)
  other arithmetic  18.2 us (3%)
  starting transfers between devices  17 us (3%)
  between operations  15.7 us (3%)
    ppermute x7, waiting for transfers between devices, on_device(): pieces.append(lax.ppermute(pieces[-1], 'tok', right))  170 us
    all_to_all x1, waiting for transfers between devices, on_device(): lax.all_to_all(partial_second, 'tok', split_axis=0, concat_axis=0, tiled=...  103 us
    dot_general x1, matrix products, on_device(): lax.dot_general(segment, weights, (((1,), (1,)), ((), ())), preferred_ele...  42.6 us
    all_gather x1, waiting for transfers between devices, layer_chain(): lax.all_gather(decoded.astype(jnp.bfloat16), 'layer', axis=0, tiled=False)  27.7 us
    dot_general x1, matrix products, on_device(): jnp.dot(spread, w_second, preferred_element_type=jnp.float32)  24 us
    dot_general x1, matrix products, on_device(): jnp.dot(spread, w_first, preferred_element_type=jnp.float32)  21.9 us
    unnamed x21, local copies, waits for them, and re-layouts  19.1 us
    reduce_scatter x1, waiting for transfers between devices, on_device(): lax.psum_scatter(partial_first, 'tok', scatter_dimension=0, tiled=True)  18.2 us
  transfers between devices with their start and end apart: 13, of which 12 were waited for; matrix products, arithmetic and copies ran while one was open for 8% of the time, Pallas kernels for 0%

profile of v1, /device:TPU:0, one launch (start us, length us, event | category | flops | bytes accessed | tf_op | source)
XLA Modules:
  0.0 527.0 jit_solution(6303029670626101970)
XLA Ops:
  8.0 0.7 fusion.42
  8.7 0.7 pad_maximum_fusion.2
  9.4 0.7 broadcast_in_dim.36
  10.1 7.3 %all-to-all-start = ((bf16[8,128,96]{1,2,0:T(8,128)(2,1)}), bf16[8,128,96]{1,2,0:T(8,128)(2,1)S(1)}, u32[]{:S(2)}, u32[]{:S(2)}) async-start(bf16[8,128,96]{1,2,0:T(8,128)(2,1)} %broadcast_in_dim.36), calls=%async_computation | async-start | bytes 393216 | tf_op jit(solution)/shard_map/all_to_all | solution.py:38
  17.4 0.0 reduce-scatter.2.cloned.1.call-start
  17.5 7.9 %all-to-all-done = bf16[8,128,96]{1,2,0:T(8,128)(2,1)S(1)} async-done(((bf16[8,128,96]{1,2,0:T(8,128)(2,1)}), bf16[8,128,96]{1,2,0:T(8,128)(2,1)S(1)}, u32[]{:S(2)}, u32[]{:S(2)}) %all-to-all-start) | async-done | bytes 196640 | tf_op jit(solution)/shard_map/all_to_all | solution.py:38
  25.4 0.2 fusion.40
  25.6 0.2 copy.17
  25.8 0.0 copy-start.1
  25.8 0.2 copy.15
  26.0 0.2 copy.16
  26.2 9.7 %fusion.15 = bf16[1024,32,128]{2,1,0:T(8,128)(2,1)S(1)} fusion(s32[1024,32]{1,0:T(8,128)S(1)} %copy.17, s32[1024,32]{1,0:T(8,128)S(1)} %copy.15, bf16[1024,32]{1,0:T(8,128)(2,1)S(1)} %copy.16), kind=kOutput, calls=%fused_computation.20 | convolution fusion | flops 278921216 | bytes 8716288 | tf_op jit(solution)/shard_map/tkh,tkl->thl/dot_general | solution.py:78
  35.9 3.2 copy-done.6
  39.2 21.9 %fusion.20 = bf16[1024,2048]{1,0:T(8,128)(2,1)} fusion(bf16[4096,4096]{1,0:T(8,128)(2,1)} %bitcast.154, bf16[128,8,32,128]{3,2,1,0:T(8,128)(2,1)S(1)} %bitcast.156), kind=kOutput, calls=%fused_computation.23 | convolution fusion | flops 17181966336 | bytes 29360128 | tf_op jit(solution)/shard_map/dot_general | solution.py:84
  61.0 0.0 reduce-scatter.2.cloned.1.call-update
  61.1 24.0 %fusion.25 = bf16[1024,2048]{1,0:T(8,128)(2,1)} fusion(bf16[4096,4096]{1,0:T(8,128)(2,1)} %bitcast.155, bf16[128,8,32,128]{3,2,1,0:T(8,128)(2,1)} %bitcast.157), kind=kOutput, calls=%fused_computation.24 | convolution fusion | flops 17181966336 | bytes 29360128 | tf_op jit(solution)/shard_map/dot_general | solution.py:88
  85.0 4.6 all-to-all-start.1
  89.6 0.0 all-gather.6.cloned.1.call-start
  89.6 0.5 all-gather.6.cloned.1.call-update
  90.2 0.0 copy-start.5
  90.2 0.2 all-gather.4.cloned.1.call-start
  90.4 103.2 %all-to-all-done.1 = bf16[8,128,2048]{2,1,0:T(8,128)(2,1)} async-done(((bf16[8,128,2048]{2,1,0:T(8,128)(2,1)}), bf16[8,128,2048]{2,1,0:T(8,128)(2,1)}, u32[]{:S(2)}, u32[]{:S(2)}) %all-to-all-start.1) | async-done | bytes 4194336 | tf_op jit(solution)/shard_map/all_to_all | solution.py:91
  193.6 3.4 convert_reduce_fusion
  197.0 0.0 copy-start
  197.0 0.1 convert_bitcast_fusion.1
  197.0 18.2 %reduce-scatter.2.cloned.1.call-done = bf16[128,2048]{1,0:T(8,128)(2,1)} async-done(((bf16[1024,2048]{1,0:T(8,128)(2,1)}), bf16[128,2048]{1,0:T(8,128)(2,1)}) %reduce-scatter.2.cloned.1.call-update) | async-done | bytes 524304 | tf_op jit(solution)/shard_map/reduce_scatter | solution.py:87
  215.3 2.1 pad_maximum_fusion.1
  217.3 0.0 all-gather.4.cloned.1.call-update
  217.4 5.2 all-gather
  222.6 1.2 convert_element_type.103
  223.8 0.0 all-gather.6.cloned.1.call-done
  223.9 27.7 %all-gather.4.cloned.1.call-done = bf16[4,128,4096]{2,1,0:T(8,128)(2,1)} async-done(((bf16[1,128,4096]{2,1,0:T(8,128)(2,1)}), bf16[4,128,4096]{2,1,0:T(8,128)(2,1)}) %all-gather.4.cloned.1.call-update) | async-done | bytes 4194320 | tf_op jit(solution)/shard_map/all_gather | solution.py:50
  251.6 5.4 %bitcast_dynamic-update-slice_fusion.7 = (bf16[8,128,4096]{2,1,0:T(8,128)(2,1)}, bf16[128,4096]{1,0:T(8,128)(2,1)S(1)}) fusion(bf16[4,128,4096]{2,1,0:T(8,128)(2,1)} %all-gather.6.cloned.1.call-done, bf16[4,128,4096]{2,1,0:T(8,128)(2,1)} %all-gather.4.cloned.1.call-done, pred[]{:T(512)S(6)} %eq.25, f32[4096]{0:T(1024)S(1)} %bitcast.143, pred[]{:T(512)S(6)} %eq.55, ...), kind=kLoop, calls=%fused_computation.61 | loop fusion | flops 19398656 | bytes 13697028
  257.0 1.5 collective-permute-start
  258.5 26.5 %collective-permute-done = bf16[128,4096]{1,0:T(8,128)(2,1)S(1)} collective-permute-done((bf16[128,4096]{1,0:T(8,128)(2,1)S(1)}, bf16[128,4096]{1,0:T(8,128)(2,1)S(1)}, u32[]{:S(2)}, u32[]{:S(2)}) %collective-permute-start) | collective-permute-done | bytes 1048608 | tf_op jit(solution)/shard_map/ppermute | solution.py:102
  285.0 0.0 collective-permute-start.1
  285.0 27.2 %collective-permute-done.1 = bf16[128,4096]{1,0:T(8,128)(2,1)S(1)} collective-permute-done((bf16[128,4096]{1,0:T(8,128)(2,1)S(1)}, bf16[128,4096]{1,0:T(8,128)(2,1)S(1)}, u32[]{:S(2)}, u32[]{:S(2)}) %collective-permute-start.1) | collective-permute-done | bytes 1048608 | tf_op jit(solution)/shard_map/ppermute | solution.py:102
  312.2 0.0 collective-permute-start.2
  312.2 26.3 %collective-permute-done.2 = bf16[128,4096]{1,0:T(8,128)(2,1)S(1)} collective-permute-done((bf16[128,4096]{1,0:T(8,128)(2,1)S(1)}, bf16[128,4096]{1,0:T(8,128)(2,1)S(1)}, u32[]{:S(2)}, u32[]{:S(2)}) %collective-permute-start.2) | collective-permute-done | bytes 1048608 | tf_op jit(solution)/shard_map/ppermute | solution.py:102
  338.5 0.0 collective-permute-start.3
  338.5 25.3 %collective-permute-done.3 = bf16[128,4096]{1,0:T(8,128)(2,1)S(1)} collective-permute-done((bf16[128,4096]{1,0:T(8,128)(2,1)S(1)}, bf16[128,4096]{1,0:T(8,128)(2,1)S(1)}, u32[]{:S(2)}, u32[]{:S(2)}) %collective-permute-start.3) | collective-permute-done | bytes 1048608 | tf_op jit(solution)/shard_map/ppermute | solution.py:102
  363.8 0.0 collective-permute-start.4
  363.8 1.0 bitcast_dynamic-update-slice_fusion.6
  364.9 1.0 bitcast_dynamic-update-slice_fusion.5
  365.9 22.3 %collective-permute-done.4 = bf16[128,4096]{1,0:T(8,128)(2,1)S(1)} collective-permute-done((bf16[128,4096]{1,0:T(8,128)(2,1)S(1)}, bf16[128,4096]{1,0:T(8,128)(2,1)S(1)}, u32[]{:S(2)}, u32[]{:S(2)}) %collective-permute-start.4) | collective-permute-done | bytes 1048608 | tf_op jit(solution)/shard_map/ppermute | solution.py:102
  388.2 0.0 collective-permute-start.5
  388.2 1.0 bitcast_dynamic-update-slice_fusion.4
  389.3 1.0 bitcast_dynamic-update-slice_fusion.3
  390.3 21.4 %collective-permute-done.5 = bf16[128,4096]{1,0:T(8,128)(2,1)S(1)} collective-permute-done((bf16[128,4096]{1,0:T(8,128)(2,1)S(1)}, bf16[128,4096]{1,0:T(8,128)(2,1)S(1)}, u32[]{:S(2)}, u32[]{:S(2)}) %collective-permute-start.5) | collective-permute-done | bytes 1048608 | tf_op jit(solution)/shard_map/ppermute | solution.py:102
  411.7 0.0 collective-permute-start.6
  411.7 1.1 bitcast_dynamic-update-slice_fusion.2
  412.8 1.1 bitcast_dynamic-update-slice_fusion.1
  413.8 20.5 %collective-permute-done.6 = bf16[128,4096]{1,0:T(8,128)(2,1)S(1)} collective-permute-done((bf16[128,4096]{1,0:T(8,128)(2,1)S(1)}, bf16[128,4096]{1,0:T(8,128)(2,1)S(1)}, u32[]{:S(2)}, u32[]{:S(2)}) %collective-permute-start.6) | collective-permute-done | bytes 1048608 | tf_op jit(solution)/shard_map/ppermute | solution.py:102
  434.3 1.1 bitcast_dynamic-update-slice_fusion
  435.4 8.1 %gather_fusion = bf16[8,128,4096]{2,1,0:T(8,128)(2,1)} fusion(bf16[8,128,4096]{2,1,0:T(8,128)(2,1)} %bitcast_dynamic-update-slice_fusion, s32[1024]{0:T(1024)S(1)} %pad_clamp_fusion), kind=kCustom, calls=%fused_computation | custom fusion | bytes 16777248 | tf_op jit(solution)/shard_map/gather | solution.py:104
  443.5 42.6 %convert_bitcast_fusion = bf16[128,8,32,128]{3,1,2,0:T(8,128)(2,1)} fusion(bf16[1024,4096]{1,0:T(8,128)(2,1)} %bitcast.138, bf16[1,4096,4096]{2,1,0:T(8,128)(2,1)} %param.8), kind=kOutput, calls=%fused_computation.13 | convolution fusion | flops 34363932672 | bytes 50331648 | tf_op jit(solution)/shard_map/dot_general | solution.py:106
  486.1 9.5 %copy.24 = bf16[128,8,32,128]{3,2,1,0:T(8,128)(2,1)} copy(bf16[128,8,32,128]{3,1,2,0:T(8,128)(2,1)} %convert_bitcast_fusion) | data formatting | bytes 16777216
  495.6 0.0 copy-done.2
  495.7 10.7 %select_reduce_fusion = f32[1024,32]{1,0:T(8,128)} fusion(s32[1024,32]{1,0:T(8,128)S(1)} %copy-done.4, bf16[1024,32,128]{2,1,0:T(8,128)(2,1)} %bitcast.139, s32[1024,32]{1,0:T(8,128)S(1)} %copy-done.2), kind=kOutput, calls=%fused_computation.5 | convolution fusion | flops 275742720 | bytes 8781824 | tf_op jit(solution)/shard_map/thl,tkl->tkh/dot_general | solution.py:110
  506.4 1.9 copy.19
  508.3 3.4 all-to-all-start.2
  511.6 3.8 fusion.39
  515.4 3.5 all-to-all-done.2
  518.9 0.6 reduce_sum.29
  (14 shorter events, 0.1 us)
Async XLA Ops:
  10.1 15.2 %all-to-all-start = ((bf16[8,128,96]{1,2,0:T(8,128)(2,1)}), bf16[8,128,96]{1,2,0:T(8,128)(2,1)S(1)}, u32[]{:S(2)}, u32[]{:S(2)}) async-start(bf16[8,128,96]{1,2,0:T(8,128)(2,1)} %broadcast_in_dim.36), calls=%async_computation | async-start | bytes 393216 | tf_op jit(solution)/shard_map/all_to_all | solution.py:38
  17.4 197.8 %reduce-scatter.2.cloned.1.call-start = ((), (), s32[]{:S(2)}) async-start(), calls=%async_computation.4 | async-start | bytes 4718592 | tf_op jit(solution)/shard_map/reduce_scatter | solution.py:87
  25.8 10.1 %copy-start.1 = (s32[1024,32]{1,0:T(8,128)}, s32[1024,32]{1,0:T(8,128)S(1)}, u32[]{:S(2)}) copy-start(s32[1024,32]{1,0:T(8,128)S(1)} %copy.17) | copy-start | bytes 393220
  26.0 9.9 %copy-start.3 = (s32[1024,32]{1,0:T(8,128)}, s32[1024,32]{1,0:T(8,128)S(1)}, u32[]{:S(2)}) copy-start(s32[1024,32]{1,0:T(8,128)S(1)} %copy.15) | copy-start | bytes 393220
  35.9 3.2 copy-start.6
  85.0 108.6 %all-to-all-start.1 = ((bf16[8,128,2048]{2,1,0:T(8,128)(2,1)}), bf16[8,128,2048]{2,1,0:T(8,128)(2,1)}, u32[]{:S(2)}, u32[]{:S(2)}) async-start(bf16[8,128,2048]{2,1,0:T(8,128)(2,1)} %bitcast.140), calls=%async_computation.2 | async-start | bytes 8388608 | tf_op jit(solution)/shard_map/all_to_all | solution.py:91
  89.6 134.3 %all-gather.6.cloned.1.call-start = ((), (), s32[]{:S(2)}) async-start(), calls=%async_computation.6 | async-start | bytes 5242880 | tf_op jit(solution)/shard_map/all_gather | solution.py:49
  90.2 127.2 %copy-start.5 = (f32[1,4096]{1,0:T(1,128)S(1)}, f32[1,4096]{1,0:T(1,128)}, u32[]{:S(2)}) copy-start(f32[1,4096]{1,0:T(1,128)} %param.9) | copy-start | bytes 49156
  90.2 161.4 %all-gather.4.cloned.1.call-start = ((), (), s32[]{:S(2)}) async-start(), calls=%async_computation.5 | async-start | bytes 5242880 | tf_op jit(solution)/shard_map/all_gather | solution.py:50
  197.0 54.6 %copy-start = (bf16[128,4096]{1,0:T(8,128)(2,1)S(1)}, bf16[128,4096]{1,0:T(8,128)(2,1)}, u32[]{:S(2)}) copy-start(bf16[128,4096]{1,0:T(8,128)(2,1)} %param.10) | copy-start | bytes 3145732
  257.0 28.0 %collective-permute-start = (bf16[128,4096]{1,0:T(8,128)(2,1)S(1)}, bf16[128,4096]{1,0:T(8,128)(2,1)S(1)}, u32[]{:S(2)}, u32[]{:S(2)}) collective-permute-start(bf16[128,4096]{1,0:T(8,128)(2,1)S(1)} %get-tuple-element.3), channel_id=1, source_target_pairs={{0,1},{1,2},{2,3},{3,4},{4,5},{5,6},{6,7},{7,0},{8,9},{9,10},{10,1... | collective-permute-start | bytes 3145736 | tf_op jit(solution)/shard_map/ppermute | solution.py:102
  285.0 27.2 %collective-permute-start.1 = (bf16[128,4096]{1,0:T(8,128)(2,1)S(1)}, bf16[128,4096]{1,0:T(8,128)(2,1)S(1)}, u32[]{:S(2)}, u32[]{:S(2)}) collective-permute-start(bf16[128,4096]{1,0:T(8,128)(2,1)S(1)} %collective-permute-done), channel_id=1, source_target_pairs={{0,1},{1,2},{2,3},{3,4},{4,5},{5,6},{6,7},{7,0},{8,9},{9,10},{10,1... | collective-permute-start | bytes 3145736 | tf_op jit(solution)/shard_map/ppermute | solution.py:102
  312.2 26.3 %collective-permute-start.2 = (bf16[128,4096]{1,0:T(8,128)(2,1)S(1)}, bf16[128,4096]{1,0:T(8,128)(2,1)S(1)}, u32[]{:S(2)}, u32[]{:S(2)}) collective-permute-start(bf16[128,4096]{1,0:T(8,128)(2,1)S(1)} %collective-permute-done.1), channel_id=1, source_target_pairs={{0,1},{1,2},{2,3},{3,4},{4,5},{5,6},{6,7},{7,0},{8,9},{9,10},{10,1... | collective-permute-start | bytes 3145736 | tf_op jit(solution)/shard_map/ppermute | solution.py:102
  338.5 25.3 %collective-permute-start.3 = (bf16[128,4096]{1,0:T(8,128)(2,1)S(1)}, bf16[128,4096]{1,0:T(8,128)(2,1)S(1)}, u32[]{:S(2)}, u32[]{:S(2)}) collective-permute-start(bf16[128,4096]{1,0:T(8,128)(2,1)S(1)} %collective-permute-done.2), channel_id=1, source_target_pairs={{0,1},{1,2},{2,3},{3,4},{4,5},{5,6},{6,7},{7,0},{8,9},{9,10},{10,1... | collective-permute-start | bytes 3145736 | tf_op jit(solution)/shard_map/ppermute | solution.py:102
  363.8 24.4 %collective-permute-start.4 = (bf16[128,4096]{1,0:T(8,128)(2,1)S(1)}, bf16[128,4096]{1,0:T(8,128)(2,1)S(1)}, u32[]{:S(2)}, u32[]{:S(2)}) collective-permute-start(bf16[128,4096]{1,0:T(8,128)(2,1)S(1)} %collective-permute-done.3), channel_id=1, source_target_pairs={{0,1},{1,2},{2,3},{3,4},{4,5},{5,6},{6,7},{7,0},{8,9},{9,10},{10,1... | collective-permute-start | bytes 3145736 | tf_op jit(solution)/shard_map/ppermute | solution.py:102
  388.2 23.5 %collective-permute-start.5 = (bf16[128,4096]{1,0:T(8,128)(2,1)S(1)}, bf16[128,4096]{1,0:T(8,128)(2,1)S(1)}, u32[]{:S(2)}, u32[]{:S(2)}) collective-permute-start(bf16[128,4096]{1,0:T(8,128)(2,1)S(1)} %collective-permute-done.4), channel_id=1, source_target_pairs={{0,1},{1,2},{2,3},{3,4},{4,5},{5,6},{6,7},{7,0},{8,9},{9,10},{10,1... | collective-permute-start | bytes 3145736 | tf_op jit(solution)/shard_map/ppermute | solution.py:102
  411.7 22.6 %collective-permute-start.6 = (bf16[128,4096]{1,0:T(8,128)(2,1)S(1)}, bf16[128,4096]{1,0:T(8,128)(2,1)S(1)}, u32[]{:S(2)}, u32[]{:S(2)}) collective-permute-start(bf16[128,4096]{1,0:T(8,128)(2,1)S(1)} %collective-permute-done.5), channel_id=1, source_target_pairs={{0,1},{1,2},{2,3},{3,4},{4,5},{5,6},{6,7},{7,0},{8,9},{9,10},{10,1... | collective-permute-start | bytes 3145736 | tf_op jit(solution)/shard_map/ppermute | solution.py:102
  486.1 9.6 %copy-start.2 = (s32[1024,32]{1,0:T(8,128)S(1)}, s32[1024,32]{1,0:T(8,128)}, u32[]{:S(2)}) copy-start(s32[1024,32]{1,0:T(8,128)} %copy-done.1) | copy-start | bytes 393220
  486.1 9.6 %copy-start.4 = (s32[1024,32]{1,0:T(8,128)S(1)}, s32[1024,32]{1,0:T(8,128)}, u32[]{:S(2)}) copy-start(s32[1024,32]{1,0:T(8,128)} %copy-done.3) | copy-start | bytes 393220
  508.3 10.7 %all-to-all-start.2 = ((f32[8,128,32]{1,2,0:T(8,128)}), f32[8,128,32]{1,2,0:T(8,128)S(1)}, u32[]{:S(2)}, u32[]{:S(2)}) async-start(f32[8,128,32]{1,2,0:T(8,128)} %copy.19), calls=%async_computation.3 | async-start | bytes 262144 | tf_op jit(solution)/shard_map/all_to_all | solution.py:114
Sparse Core Ops, SparseCore 0:
  61.2 154.0 reduce-scatter.1
Sparse Core Ops, SparseCore 1:
  91.7 35.6 all-gather.5
  217.5 34.1 all-gather.3
